TPU v7x, 32 devices: a whole 2x2x4 slice. The times are simulated.
32 devices in a mesh: groups: 2 (over y), lat: 16 (over z, x, core).
Axes of the slice: x: 2, y: 2, z: 4, core: 2. Of those that a mesh axis runs over, the one named last changes fastest.
Arguments:
- latent: bfloat16 [16384, 1536], P(('groups', 'lat')), parts along dimension 0, may hold values from -400 to 400
- query_gain: float32 [1536], replicated, may hold values from 0.1 to 1.9
- key_gain: float32 [1536], replicated, may hold values from 0.1 to 1.9
- output_gain: float32 [1536], replicated, may hold values from 0.1 to 1.9
- output_weight: bfloat16 [1536, 1536], replicated, may hold values from -0.15625 to 0.15625
- observations: bfloat16 [128, 128, 128], P(('groups', 'lat')), parts along dimension 0, may hold values from -6 to 6
- panels: bfloat16 [1024, 1536], P('lat'), may hold values from -0.5 to 0.5
- instrument: int32 [128], P('groups'), parts along dimension 0, may hold values from 0 to 7
- observed_count: int32 [128], P('groups'), parts along dimension 0, may hold values from 1 to 128
- footprint: int32 [128, 6], P(('groups', 'lat')), parts along dimension 0, may hold values from 0 to 63, as said below
- tile_blocks: int32 [128], P(('groups', 'lat')), parts along dimension 0, may hold values from 1 to 6
Outputs:
- encoded: bfloat16 [16384, 1536], P(('groups', 'lat')), parts along dimension 0
There are 2 independent parts, one for each index of `groups`. A program takes and returns all parts, laid end to end along the dimension named above; an argument that names none is the same for every part. Nothing has to cross between parts.
Inputs may be any that keep to these rules, and one draw needn't show every extreme that they name: `footprint`: tile t lies on latitude device t // 4 and block b on b // 4; every entry of tile t's list names a block on that device or on one of the two beside it.
All inputs are finite; a program needn't handle non-finite values.
Results may differ from a plain program's by a relative error of at most 0.0039.
Values may be sent and summed in bfloat16 or wider, within the bound.
No kernel may reach another device: no remote copies, remote signals or barrier semaphores. Data moves between devices by JAX's collectives and lax.ppermute only.
A program may use at most 128 MiB of HBM per device.

v0:
```python
import math
import jax
import jax.numpy as jnp
from jax import lax
from jax.sharding import PartitionSpec as P

D = 1536
HD = 64
NINST = 8
CH = 128
CELLS = 128
OBS = 128
MAXB = 6


def padded(value, sides, width):
    for axis, dim in sides:
        peers, length = (lax.axis_size(axis), value.shape[dim])
        up = [(i, (i + 1) % peers) for i in range(peers - 1)]
        down = [(j, i) for i, j in up]
        last = lax.slice_in_dim(value, length - width, length, axis=dim)
        first = lax.slice_in_dim(value, 0, width, axis=dim)
        before = lax.ppermute(last, axis, up)
        after = lax.ppermute(first, axis, down)
        value = jnp.concatenate([before, value, after], axis=dim)
    return value


def normalize(values, gain):
    values = values.astype(jnp.float32)
    return values * lax.rsqrt(jnp.mean(values * values, axis=-1, keepdims=True) + 1e-06) * gain


def body(
    latent,
    query_gain,
    key_gain,
    output_gain,
    output_weight,
    observations,
    panels,
    instrument,
    observed_count,
    footprint,
    tile_blocks,
):
    block_count = observations.shape[0]
    position = lax.axis_index("lat")
    first_block = (position - 1) * block_count
    all_blocks = instrument.shape[0]
    table = lax.all_gather(panels, "lat", axis=0, tiled=True)
    near_count = 3 * block_count
    near_ids = jnp.clip(first_block + jnp.arange(near_count, dtype=jnp.int32), 0, all_blocks - 1)
    kind_range = jnp.arange(NINST, dtype=jnp.int32)
    own_kinds = lax.dynamic_slice_in_dim(instrument, position * block_count, block_count)
    select = (own_kinds[:, None] == kind_range[None, :]).astype(jnp.bfloat16)
    widened = (observations[:, :, None, :] * select[:, None, :, None]).reshape(
        observations.shape[0], OBS, NINST * CH
    )
    embedded = jnp.einsum("bop,pd->bod", widened, table, preferred_element_type=jnp.float32).astype(
        jnp.bfloat16
    )
    nearby = padded(embedded, (("lat", 0),), block_count)
    keys = normalize(nearby, key_gain).astype(jnp.bfloat16)
    counts = observed_count[near_ids]
    tiles = latent.shape[0] // CELLS
    heads = D // HD
    keys_t = keys.reshape(near_count, OBS, heads, HD).transpose(0, 2, 3, 1)
    values_t = nearby.reshape(near_count, OBS, heads, HD).transpose(0, 2, 3, 1)
    queries = (latent.astype(jnp.float32) * query_gain).astype(jnp.bfloat16)
    queries_t = queries.reshape(tiles, CELLS, heads, HD).transpose(0, 2, 3, 1)
    local_ids = footprint - first_block
    scale = 1.0 / math.sqrt(HD)
    slot_rows = jnp.arange(OBS, dtype=jnp.int32)
    near_range = jnp.arange(near_count, dtype=jnp.int32)

    def attend(slot_index, carry):
        running, total, accum = carry
        chosen = lax.dynamic_index_in_dim(local_ids, slot_index, 1, keepdims=False)
        pick = chosen[:, None] == near_range[None, :]
        select = pick.astype(jnp.bfloat16)
        slot_keys = jnp.einsum(
            "tn,nhdk->thdk", select, keys_t, preferred_element_type=jnp.float32
        ).astype(jnp.bfloat16)
        slot_values = jnp.einsum(
            "tn,nhdk->thdk", select, values_t, preferred_element_type=jnp.float32
        ).astype(jnp.bfloat16)
        slot_counts = jnp.sum(jnp.where(pick, counts[None, :], 0), axis=1)
        scores = (
            jnp.einsum("thdq,thdk->thqk", queries_t, slot_keys, preferred_element_type=jnp.float32)
            * scale
        )
        usable = (slot_index < tile_blocks)[:, None] & (slot_rows[None, :] < slot_counts[:, None])
        usable = usable[:, None, None, :]
        highest = jnp.maximum(running, jnp.max(jnp.where(usable, scores, -1e30), axis=-1))
        factor = jnp.exp(running - highest)
        weights = jnp.where(usable, jnp.exp(scores - highest[..., None]), 0.0)
        total = total * factor + jnp.sum(weights, axis=-1)
        update = jnp.einsum(
            "thdk,thqk->thdq",
            slot_values,
            weights.astype(jnp.bfloat16),
            preferred_element_type=jnp.float32,
        )
        accum = accum * factor[:, :, None, :] + update
        return (highest, total, accum)

    start = (
        jnp.full((tiles, heads, CELLS), -1e30, jnp.float32),
        jnp.zeros((tiles, heads, CELLS), jnp.float32),
        jnp.zeros((tiles, heads, HD, CELLS), jnp.float32),
    )
    running, total, accum = lax.fori_loop(0, MAXB, attend, start)
    attended = (
        (accum / total[:, :, None, :])
        .astype(jnp.bfloat16)
        .transpose(0, 3, 1, 2)
        .reshape(tiles * CELLS, D)
    )
    mixed = latent.astype(jnp.float32) + jnp.dot(
        attended, output_weight, preferred_element_type=jnp.float32
    )
    return normalize(mixed, output_gain).astype(jnp.bfloat16)


def solution(mesh):
    return jax.shard_map(
        body,
        mesh=mesh,
        in_specs=(
            P(("groups", "lat"), None),
            P(),
            P(),
            P(),
            P(),
            P(("groups", "lat"), None, None),
            P("lat", None),
            P("groups"),
            P("groups"),
            P(("groups", "lat"), None),
            P(("groups", "lat")),
        ),
        out_specs=P(("groups", "lat"), None),
        check_vma=False,
    )
```

profile of v0, /device:TPU:1, one launch (start us, length us, event | category | flops | bytes accessed | tf_op | source)
XLA Modules:
  0.0 224.9 jit_solution(17268411297548896115)
XLA Ops:
  9.7 47.9 %all-gather.2.cloned.1.call-done = bf16[1024,1536]{1,0:T(8,128)(2,1)} async-done(((bf16[64,1536]{1,0:T(8,128)(2,1)}), bf16[1024,1536]{1,0:T(8,128)(2,1)}) %all-gather.2.cloned.1.call-update) | async-done | bytes 3145744 | tf_op jit(solution)/shard_map/all_gather | solution.py:51
  57.6 5.0 %fusion.30 = bf16[4,128,1536]{2,1,0:T(8,128)(2,1)} fusion(bf16[1024,1536]{1,0:T(8,128)(2,1)} %all-gather.2.cloned.1.call-done, bf16[4,128,1024]{2,1,0:T(8,128)(2,1)S(1)} %mul.113, bf16[4,1024]{1,0:T(4,128)(2,1)S(1)} %bitcast.76), kind=kOutput, calls=%fused_computation.47 | convolution fusion | flops 1611923456 | bytes 5775360 | tf_op jit(solution)/shard_map/bop,pd->bod/dot_general | solution.py:60
  62.5 2.2 collective-permute-start.1
  64.7 3.4 %collective-permute-start = (bf16[4,128,1536]{2,1,0:T(8,128)(2,1)}, bf16[4,128,1536]{2,1,0:T(8,128)(2,1)}, u32[]{:S(2)}, u32[]{:S(2)}) collective-permute-start(bf16[4,128,1536]{2,1,0:T(8,128)(2,1)} %fusion.30), channel_id=1, source_target_pairs={{0,1},{1,2},{2,3},{3,4},{4,5},{5,6},{6,7},{7,8},{8,9},{9,10},{10,1... | collective-permute-start | bytes 4718600 | tf_op jit(solution)/shard_map/ppermute | solution.py:23
  70.9 1.9 copy.33
  72.8 11.8 %collective-permute-done.1 = bf16[4,128,1536]{2,1,0:T(8,128)(2,1)} collective-permute-done((bf16[4,128,1536]{2,1,0:T(8,128)(2,1)}, bf16[4,128,1536]{2,1,0:T(8,128)(2,1)}, u32[]{:S(2)}, u32[]{:S(2)}) %collective-permute-start.1) | collective-permute-done | bytes 1572896 | tf_op jit(solution)/shard_map/ppermute | solution.py:24
  84.6 16.1 %collective-permute-done = bf16[4,128,1536]{2,1,0:T(8,128)(2,1)} collective-permute-done((bf16[4,128,1536]{2,1,0:T(8,128)(2,1)}, bf16[4,128,1536]{2,1,0:T(8,128)(2,1)}, u32[]{:S(2)}, u32[]{:S(2)}) %collective-permute-start) | collective-permute-done | bytes 1572896 | tf_op jit(solution)/shard_map/ppermute | solution.py:23
  100.7 5.7 %multiply_reduce_fusion = (f32[12,128]{1,0:T(8,128)S(1)}, bf16[12,128,1536]{2,1,0:T(8,128)(2,1)}) fusion(bf16[4,128,1536]{2,1,0:T(8,128)(2,1)} %collective-permute-done.1, bf16[4,128,1536]{2,1,0:T(8,128)(2,1)} %fusion.30, bf16[4,128,1536]{2,1,0:T(8,128)(2,1)} %collective-permute-done), kind=kLoop, calls=%fused_computation.36 | loop fusion | flops 11794944 | bytes 9443328 | tf_op jit(solution)/shard_map/reduce_sum | solution.py:31
  106.4 2.6 %copy.34 = bf16[4,128,1536]{1,2,0:T(8,128)(2,1)} copy(bf16[4,128,1536]{2,1,0:T(8,128)(2,1)} %collective-permute-done.1) | data formatting | bytes 3145728 | tf_op jit(solution)/shard_map/ppermute | solution.py:24
  109.0 2.6 %copy.32 = bf16[4,128,1536]{1,2,0:T(8,128)(2,1)} copy(bf16[4,128,1536]{2,1,0:T(8,128)(2,1)} %collective-permute-done) | data formatting | bytes 3145728 | tf_op jit(solution)/shard_map/ppermute | solution.py:23
  111.6 3.7 %fusion.26 = bf16[12,24,64,128]{3,2,1,0:T(8,128)(2,1)S(1)} fusion(bf16[4,128,24,64]{1,3,2,0:T(8,128)(2,1)} %bitcast.73, bf16[4,128,24,64]{1,3,2,0:T(8,128)(2,1)S(1)} %bitcast.72, bf16[4,128,24,64]{1,3,2,0:T(8,128)(2,1)} %bitcast.74, f32[24,64]{1,0:T(8,128)S(1)} %mul.122, f32[12,128]{1,0:T(8,128)S(1)} %add_rsqrt_fusion), kind=kLoop, calls=%fused_computation.37 | loop fusion | flops 14155776 | bytes 9449472 | tf_op jit(solution)/shard_map/transpose | solution.py:68
  115.2 6.9 %copy.37 = bf16[12,24,64,128]{3,0,2,1:T(8,128)(2,1)} copy(bf16[12,24,64,128]{3,2,1,0:T(8,128)(2,1)S(1)} %fusion.26) | data formatting | bytes 9437184
  122.2 9.1 %copy.43 = bf16[12,128,1536]{1,0,2:T(8,128)(2,1)} copy(bf16[12,128,1536]{2,1,0:T(8,128)(2,1)} %get-tuple-element.287) | data formatting | bytes 9437184 | tf_op jit(solution)/shard_map/transpose | solution.py:69
  131.3 78.2 %while.18 = (s32[]{:T(128)}, f32[4,24,128]{2,1,0:T(8,128)S(1)}, f32[4,24,128]{2,1,0:T(8,128)S(1)}, f32[4,24,64,128]{3,2,1,0:T(8,128)}, s32[4]{0:T(128)S(1)}, /*i...) while((s32[]{:T(128)}, f32[4,24,128]{2,1,0:T(8,128)S(1)}, ...), condition=%wide.region_5.6_spmd.clone, body=%wide.region_1.5_spmd.clone.sunk | while | flops 461698304 | bytes 87296416 | solution.py:113
  131.6 4.0 %convolution_convert_fusion.5 = bf16[4,24,64,128]{3,0,2,1:T(4,128)(2,1)S(1)} fusion(bf16[12,24,64,128]{3,0,2,1:T(8,128)(2,1)} %get-tuple-element.394, s32[4]{0:T(128)S(1)} %dynamic-slice_bitcast_fusion.2), kind=kOutput, calls=%fused_computation.14.clone.1 | convolution fusion | flops 19660848 | bytes 6291472 | tf_op jit(solution)/shard_map/while/body/eval_jaxpr/tn,nhdk->thdk/dot_general | solution.py:85
  137.2 1.8 select_reduce_fusion.2
  140.9 1.8 fusion.63
  144.6 4.0 %convolution_convert_fusion.5 = bf16[4,24,64,128]{3,0,2,1:T(4,128)(2,1)S(1)} fusion(bf16[12,24,64,128]{3,0,2,1:T(8,128)(2,1)} %get-tuple-element.394, s32[4]{0:T(128)S(1)} %dynamic-slice_bitcast_fusion.2), kind=kOutput, calls=%fused_computation.14.clone.1 | convolution fusion | flops 19660848 | bytes 6291472 | tf_op jit(solution)/shard_map/while/body/eval_jaxpr/tn,nhdk->thdk/dot_general | solution.py:85
  150.2 1.8 select_reduce_fusion.2
  153.9 1.8 fusion.63
  157.6 4.0 %convolution_convert_fusion.5 = bf16[4,24,64,128]{3,0,2,1:T(4,128)(2,1)S(1)} fusion(bf16[12,24,64,128]{3,0,2,1:T(8,128)(2,1)} %get-tuple-element.394, s32[4]{0:T(128)S(1)} %dynamic-slice_bitcast_fusion.2), kind=kOutput, calls=%fused_computation.14.clone.1 | convolution fusion | flops 19660848 | bytes 6291472 | tf_op jit(solution)/shard_map/while/body/eval_jaxpr/tn,nhdk->thdk/dot_general | solution.py:85
  163.3 1.8 select_reduce_fusion.2
  167.0 1.8 fusion.63
  170.7 4.0 %convolution_convert_fusion.5 = bf16[4,24,64,128]{3,0,2,1:T(4,128)(2,1)S(1)} fusion(bf16[12,24,64,128]{3,0,2,1:T(8,128)(2,1)} %get-tuple-element.394, s32[4]{0:T(128)S(1)} %dynamic-slice_bitcast_fusion.2), kind=kOutput, calls=%fused_computation.14.clone.1 | convolution fusion | flops 19660848 | bytes 6291472 | tf_op jit(solution)/shard_map/while/body/eval_jaxpr/tn,nhdk->thdk/dot_general | solution.py:85
  180.0 1.8 fusion.63
  183.7 4.0 %convolution_convert_fusion.5 = bf16[4,24,64,128]{3,0,2,1:T(4,128)(2,1)S(1)} fusion(bf16[12,24,64,128]{3,0,2,1:T(8,128)(2,1)} %get-tuple-element.394, s32[4]{0:T(128)S(1)} %dynamic-slice_bitcast_fusion.2), kind=kOutput, calls=%fused_computation.14.clone.1 | convolution fusion | flops 19660848 | bytes 6291472 | tf_op jit(solution)/shard_map/while/body/eval_jaxpr/tn,nhdk->thdk/dot_general | solution.py:85
  189.3 1.8 select_reduce_fusion.2
  193.0 1.8 fusion.63
  196.8 4.0 %convolution_convert_fusion.5 = bf16[4,24,64,128]{3,0,2,1:T(4,128)(2,1)S(1)} fusion(bf16[12,24,64,128]{3,0,2,1:T(8,128)(2,1)} %get-tuple-element.394, s32[4]{0:T(128)S(1)} %dynamic-slice_bitcast_fusion.2), kind=kOutput, calls=%fused_computation.14.clone.1 | convolution fusion | flops 19660848 | bytes 6291472 | tf_op jit(solution)/shard_map/while/body/eval_jaxpr/tn,nhdk->thdk/dot_general | solution.py:85
  206.1 1.8 fusion.63
  209.5 2.5 %fusion.35 = bf16[4,128,24,64]{1,3,2,0:T(8,128)(2,1)S(1)} fusion(f32[4,24,64,128]{3,2,1,0:T(8,128)} %get-tuple-element.205, f32[4,24,128]{2,1,0:T(8,128)S(1)} %get-tuple-element.206), kind=kLoop, calls=%fused_computation.50 | loop fusion | flops 1572864 | bytes 4767744 | tf_op jit(solution)/shard_map/transpose | solution.py:117
  213.5 3.0 %multiply_reduce_fusion.1 = (f32[512]{0:T(512)S(1)}, f32[512,1536]{1,0:T(8,128)S(1)}) fusion(bf16[1536,1536]{1,0:T(8,128)(2,1)S(1)} %copy-done.11, bf16[192,8,4,128]{3,2,1,0:T(4,128)(2,1)S(1)} %bitcast.75, bf16[512,1536]{1,0:T(8,128)(2,1)S(1)} %copy-done.6), kind=kOutput, calls=%fused_computation.45 | convolution fusion | flops 2419064320 | bytes 11012096 | tf_op jit(solution)/shard_map/dot_general | solution.py:120
  (137 shorter events, 44.8 us)
Async XLA Ops:
  6.5 63.6 %copy-start = (s32[64]{0:T(128)S(1)}, s32[64]{0:T(128)}, u32[]{:S(2)}) copy-start(s32[64]{0:T(128)} %param.21) | copy-start | bytes 772
  6.5 51.0 %all-gather.2.cloned.1.call-start = ((), (), s32[]{:S(2)}) async-start(), calls=%async_computation | async-start | bytes 3342336 | tf_op jit(solution)/shard_map/all_gather | solution.py:51
  57.6 10.6 %copy-start.10 = (s32[4,6]{1,0:T(4,128)S(1)}, s32[4,6]{1,0:T(4,128)}, u32[]{:S(2)}) copy-start(s32[4,6]{1,0:T(4,128)} %param.22) | copy-start | bytes 292
  57.6 10.7 %copy-start.9 = (f32[1536]{0:T(1024)S(1)}, f32[1536]{0:T(1024)}, u32[]{:S(2)}) copy-start(f32[1536]{0:T(1024)} %param.15) | copy-start | bytes 18436
  57.6 10.7 %copy-start.5 = (bf16[512,1536]{1,0:T(8,128)(2,1)S(1)}, bf16[512,1536]{1,0:T(8,128)(2,1)}, u32[]{:S(2)}) copy-start(bf16[512,1536]{1,0:T(8,128)(2,1)} %param.13) | copy-start | bytes 4718596
  57.6 10.7 %copy-start.7 = (f32[1536]{0:T(1024)S(1)}, f32[1536]{0:T(1024)}, u32[]{:S(2)}) copy-start(f32[1536]{0:T(1024)} %param.14) | copy-start | bytes 18436
  62.5 22.0 %collective-permute-start.1 = (bf16[4,128,1536]{2,1,0:T(8,128)(2,1)}, bf16[4,128,1536]{2,1,0:T(8,128)(2,1)}, u32[]{:S(2)}, u32[]{:S(2)}) collective-permute-start(bf16[4,128,1536]{2,1,0:T(8,128)(2,1)} %fusion.30), channel_id=1, source_target_pairs={{1,0},{2,1},{3,2},{4,3},{5,4},{6,5},{7,6},{8,7},{9,8},{10,9},{11,1... | collective-permute-start | bytes 4718600 | tf_op jit(solution)/shard_map/ppermute | solution.py:24
  64.7 36.0 %collective-permute-start = (bf16[4,128,1536]{2,1,0:T(8,128)(2,1)}, bf16[4,128,1536]{2,1,0:T(8,128)(2,1)}, u32[]{:S(2)}, u32[]{:S(2)}) collective-permute-start(bf16[4,128,1536]{2,1,0:T(8,128)(2,1)} %fusion.30), channel_id=1, source_target_pairs={{0,1},{1,2},{2,3},{3,4},{4,5},{5,6},{6,7},{7,8},{8,9},{9,10},{10,1... | collective-permute-start | bytes 4718600 | tf_op jit(solution)/shard_map/ppermute | solution.py:23
  122.2 9.1 %copy-start.12 = (s32[4]{0:T(128)S(1)}, s32[4]{0:T(128)}, u32[]{:S(2)}) copy-start(s32[4]{0:T(128)} %param.23) | copy-start | bytes 52
  131.5 4.6 %copy-start.2 = (bf16[12,24,64,128]{3,0,2,1:T(8,128)(2,1)S(1)}, bf16[12,24,64,128]{3,0,2,1:T(8,128)(2,1)}, u32[]{:S(2)}) copy-start(bf16[12,24,64,128]{3,0,2,1:T(8,128)(2,1)} %get-tuple-element.392) | copy-start | bytes 14155780 | tf_op jit(solution)/shard_map/while
  139.0 1.9 copy-start.3
  142.7 1.6 copy-start.4
  144.6 4.6 %copy-start.2 = (bf16[12,24,64,128]{3,0,2,1:T(8,128)(2,1)S(1)}, bf16[12,24,64,128]{3,0,2,1:T(8,128)(2,1)}, u32[]{:S(2)}) copy-start(bf16[12,24,64,128]{3,0,2,1:T(8,128)(2,1)} %get-tuple-element.392) | copy-start | bytes 14155780 | tf_op jit(solution)/shard_map/while
  152.0 1.9 copy-start.3
  155.7 1.6 copy-start.4
  157.6 4.6 %copy-start.2 = (bf16[12,24,64,128]{3,0,2,1:T(8,128)(2,1)S(1)}, bf16[12,24,64,128]{3,0,2,1:T(8,128)(2,1)}, u32[]{:S(2)}) copy-start(bf16[12,24,64,128]{3,0,2,1:T(8,128)(2,1)} %get-tuple-element.392) | copy-start | bytes 14155780 | tf_op jit(solution)/shard_map/while
  165.1 1.9 copy-start.3
  168.8 1.6 copy-start.4
  170.7 4.6 %copy-start.2 = (bf16[12,24,64,128]{3,0,2,1:T(8,128)(2,1)S(1)}, bf16[12,24,64,128]{3,0,2,1:T(8,128)(2,1)}, u32[]{:S(2)}) copy-start(bf16[12,24,64,128]{3,0,2,1:T(8,128)(2,1)} %get-tuple-element.392) | copy-start | bytes 14155780 | tf_op jit(solution)/shard_map/while
  178.1 1.9 copy-start.3
  181.8 1.6 copy-start.4
  183.7 4.6 %copy-start.2 = (bf16[12,24,64,128]{3,0,2,1:T(8,128)(2,1)S(1)}, bf16[12,24,64,128]{3,0,2,1:T(8,128)(2,1)}, u32[]{:S(2)}) copy-start(bf16[12,24,64,128]{3,0,2,1:T(8,128)(2,1)} %get-tuple-element.392) | copy-start | bytes 14155780 | tf_op jit(solution)/shard_map/while
  191.1 1.9 copy-start.3
  194.8 1.6 copy-start.4
  196.7 4.6 %copy-start.2 = (bf16[12,24,64,128]{3,0,2,1:T(8,128)(2,1)S(1)}, bf16[12,24,64,128]{3,0,2,1:T(8,128)(2,1)}, u32[]{:S(2)}) copy-start(bf16[12,24,64,128]{3,0,2,1:T(8,128)(2,1)} %get-tuple-element.392) | copy-start | bytes 14155780 | tf_op jit(solution)/shard_map/while
  204.2 1.9 copy-start.3
  207.9 1.6 copy-start.4
  209.5 4.0 %copy-start.6 = (bf16[512,1536]{1,0:T(8,128)(2,1)S(1)}, bf16[512,1536]{1,0:T(8,128)(2,1)}, u32[]{:S(2)}) copy-start(bf16[512,1536]{1,0:T(8,128)(2,1)} %param.13) | copy-start | bytes 4718596
  209.5 4.0 %copy-start.11 = (bf16[1536,1536]{1,0:T(8,128)(2,1)S(1)}, bf16[1536,1536]{1,0:T(8,128)(2,1)}, u32[]{:S(2)}) copy-start(bf16[1536,1536]{1,0:T(8,128)(2,1)} %param.17) | copy-start | bytes 14155780
  213.5 3.0 %copy-start.8 = (f32[1536]{0:T(1024)S(1)}, f32[1536]{0:T(1024)}, u32[]{:S(2)}) copy-start(f32[1536]{0:T(1024)} %param.16) | copy-start | bytes 18436
  213.5 4.5 %copy-start.1 = (s32[64]{0:T(128)S(1)}, s32[64]{0:T(128)}, u32[]{:S(2)}) copy-start(s32[64]{0:T(128)} %param.21) | copy-start | bytes 772
Sparse Core Ops, SparseCore 0:
  9.6 47.9 all-gather.1
where the time goes:
time: 226 us; the launch traced here: 225 us
  waiting for transfers between devices  76.5 us (34%)
  matrix products  59.3 us (26%)
  local copies, waits for them, and re-layouts  43.7 us (19%)
  other arithmetic  25.7 us (11%)
  between operations  13.6 us (6%)
  starting transfers between devices  5.56 us (2%)
    all_gather x1, waiting for transfers between devices, body(): table = lax.all_gather(panels, 'lat', axis=0, tiled=True)  47.9 us
    dot_general x6, matrix products, attend(): jnp.einsum('tn,nhdk->thdk', select, values_t, preferred_element_type=jnp....  23.8 us
    ppermute x1, waiting for transfers between devices, padded(): before = lax.ppermute(last, axis, up)  16.1 us
    while x42, local copies, waits for them, and re-layouts  14.5 us
    ppermute x1, waiting for transfers between devices, padded(): after = lax.ppermute(first, axis, down)  11.8 us
    dot_general x6, matrix products, attend(): jnp.einsum('thdk,thqk->thdq', slot_values, weights.astype(jnp.bfloat16),...  10.8 us
    dot_general x6, matrix products, attend(): jnp.einsum('thdq,thdk->thqk', queries_t, slot_keys, preferred_element_typ...  10.7 us
    reduce_sum x6, other arithmetic, attend(): total = total * factor + jnp.sum(weights, axis=-1)  10 us
  transfers between devices with their start and end apart: 3, of which 3 were waited for; matrix products, arithmetic and copies ran while one was open for 3% of the time, Pallas kernels for 0%

commit v1 on v0

--- a/solution.py
+++ b/solution.py
@@ -11,6 +11,29 @@
 CELLS = 128
 OBS = 128
 MAXB = 6
+
+
+def render_the_frames(array_here, group_axis):
+    value_now = lax.axis_index(group_axis)
+    finding = lax.axis_size(group_axis)
+    low, local_next, tile_out = (finding, value_now, array_here.shape[0])
+    entries = tuple((pp * low if num == 0 else pp for num, pp in enumerate(array_here.shape)))
+    t_next = jnp.zeros(entries, array_here.dtype)
+    upper = lax.dynamic_update_slice_in_dim(t_next, array_here, local_next * tile_out, axis=0)
+    r1 = v1 = array_here
+    for p in range(1, low // 2 + 1):
+        current_value = tuple(((num, (num + 1) % low) for num in range(low)))
+        r1 = lax.ppermute(r1, axis_name=group_axis, perm=current_value)
+        upper = lax.dynamic_update_slice_in_dim(
+            upper, r1, (local_next - p) % low * tile_out, axis=0
+        )
+        if 2 * p < low:
+            then = tuple(((num, (num - 1) % low) for num in range(low)))
+            v1 = lax.ppermute(v1, axis_name=group_axis, perm=then)
+            upper = lax.dynamic_update_slice_in_dim(
+                upper, v1, (local_next + p) % low * tile_out, axis=0
+            )
+    return upper
 
 
 def padded(value, sides, width):
@@ -48,7 +71,7 @@
     position = lax.axis_index("lat")
     first_block = (position - 1) * block_count
     all_blocks = instrument.shape[0]
-    table = lax.all_gather(panels, "lat", axis=0, tiled=True)
+    table = render_the_frames(panels, "lat")
     near_count = 3 * block_count
     near_ids = jnp.clip(first_block + jnp.arange(near_count, dtype=jnp.int32), 0, all_blocks - 1)
     kind_range = jnp.arange(NINST, dtype=jnp.int32)

time: 226 us -> 213 us (0.942)
  starting transfers between devices: 5.56 us -> 47.4 us
  waiting for transfers between devices: 76.5 us -> 36.8 us
  between operations: 13.6 us -> 0.45 us
    all_gather x1 -> x0, waiting for transfers between devices: 47.9 us -> none  [body(): table = lax.all_gather(panels, 'lat', axis=0, tiled=True)]
    ppermute x0 -> x15, starting transfers between devices: none -> 36.6 us  [the longest x7 32.5 us: render_the_frames(): v1 = lax.ppermute(v1, axis_name=group_axis, perm=then)]
    ppermute x0 -> x15, waiting for transfers between devices: none -> 21.7 us  [the longest x8 13.3 us: render_the_frames(): r1 = lax.ppermute(r1, axis_name=group_axis, perm=current_value)]
    ppermute x1, waiting for transfers between devices: 16.1 us -> 8.56 us  [padded(): before = lax.ppermute(last, axis, up)]
    ppermute x1, starting transfers between devices: 2.17 us -> 8.75 us  [padded(): after = lax.ppermute(first, axis, down)]
    ppermute x1, waiting for transfers between devices: 11.8 us -> 6.51 us  [padded(): after = lax.ppermute(first, axis, down)]
    unnamed x25 -> x27, local copies, waits for them, and re-layouts: 7.56 us -> 7.56 us
  transfers between devices with their start and end apart: 3 -> 17, of which waited for: 3 -> 10; matrix products, arithmetic and copies ran while one was open for 3% -> 4% of each run, Pallas kernels for 0% -> 0%
where the time goes in v1:
time: 213 us; the launch traced here: 212 us
  matrix products  57.4 us (27%)
  starting transfers between devices  47.4 us (22%)
  local copies, waits for them, and re-layouts  44.3 us (21%)
  waiting for transfers between devices  36.8 us (17%)
  other arithmetic  25.6 us (12%)
    ppermute x7, starting transfers between devices, render_the_frames(): v1 = lax.ppermute(v1, axis_name=group_axis, perm=then)  32.5 us
    dot_general x6, matrix products, attend(): jnp.einsum('tn,nhdk->thdk', select, values_t, preferred_element_type=jnp....  23.8 us
    while x42, local copies, waits for them, and re-layouts  14.4 us
    ppermute x8, waiting for transfers between devices, render_the_frames(): r1 = lax.ppermute(r1, axis_name=group_axis, perm=current_value)  13.3 us
    dot_general x6, matrix products, attend(): jnp.einsum('thdk,thqk->thdq', slot_values, weights.astype(jnp.bfloat16),...  10.8 us
    dot_general x6, matrix products, attend(): jnp.einsum('thdq,thdk->thqk', queries_t, slot_keys, preferred_element_typ...  10.7 us
    reduce_sum x6, other arithmetic, attend(): total = total * factor + jnp.sum(weights, axis=-1)  10 us
    transpose x1, local copies, waits for them, and re-layouts, body(): values_t = nearby.reshape(near_count, OBS, heads, HD).transpose(0, 2, 3, 1)  9.12 us
  transfers between devices with their start and end apart: 17, of which 10 were waited for; matrix products, arithmetic and copies ran while one was open for 4% of the time, Pallas kernels for 0%

profile of v1, /device:TPU:1, one launch (start us, length us, event | category | flops | bytes accessed | tf_op | source)
XLA Modules:
  0.0 212.4 jit_solution(10289929910125441494)
XLA Ops:
  0.0 2.6 %collective-permute-start = (bf16[64,1536]{1,0:T(8,128)(2,1)}, bf16[64,1536]{1,0:T(8,128)(2,1)S(1)}, u32[]{:S(2)}, u32[]{:S(2)}) collective-permute-start(bf16[64,1536]{1,0:T(8,128)(2,1)} %param.19), channel_id=1, source_target_pairs={{0,1},{1,2},{2,3},{3,4},{4,5},{5,6},{6,7},{7,8},{8,9},{9,10},{10,1... | collective-permute-start | bytes 589832 | tf_op jit(solution)/shard_map/ppermute | solution.py:26
  6.2 2.8 %collective-permute-start.3 = (bf16[64,1536]{1,0:T(8,128)(2,1)S(1)}, bf16[64,1536]{1,0:T(8,128)(2,1)S(1)}, u32[]{:S(2)}, u32[]{:S(2)}) collective-permute-start(bf16[64,1536]{1,0:T(8,128)(2,1)S(1)} %collective-permute-done.1), channel_id=1, source_target_pairs={{0,15},{1,0},{2,1},{3,2},{4,3},{5,4},{6,5},{7,6},{8,7},{9,8},{10,9... | collective-permute-start | bytes 589832 | tf_op jit(solution)/shard_map/ppermute | solution.py:32
  10.1 3.2 %collective-permute-done.3 = bf16[64,1536]{1,0:T(8,128)(2,1)S(1)} collective-permute-done((bf16[64,1536]{1,0:T(8,128)(2,1)S(1)}, bf16[64,1536]{1,0:T(8,128)(2,1)S(1)}, u32[]{:S(2)}, u32[]{:S(2)}) %collective-permute-start.3) | collective-permute-done | bytes 196640 | tf_op jit(solution)/shard_map/ppermute | solution.py:32
  13.4 3.3 %collective-permute-start.5 = (bf16[64,1536]{1,0:T(8,128)(2,1)S(1)}, bf16[64,1536]{1,0:T(8,128)(2,1)S(1)}, u32[]{:S(2)}, u32[]{:S(2)}) collective-permute-start(bf16[64,1536]{1,0:T(8,128)(2,1)S(1)} %collective-permute-done.3), channel_id=1, source_target_pairs={{0,15},{1,0},{2,1},{3,2},{4,3},{5,4},{6,5},{7,6},{8,7},{9,8},{10,9... | collective-permute-start | bytes 589832 | tf_op jit(solution)/shard_map/ppermute | solution.py:32
  18.5 6.0 %collective-permute-start.7 = (bf16[64,1536]{1,0:T(8,128)(2,1)S(1)}, bf16[64,1536]{1,0:T(8,128)(2,1)S(1)}, u32[]{:S(2)}, u32[]{:S(2)}) collective-permute-start(bf16[64,1536]{1,0:T(8,128)(2,1)S(1)} %collective-permute-done.5), channel_id=1, source_target_pairs={{0,15},{1,0},{2,1},{3,2},{4,3},{5,4},{6,5},{7,6},{8,7},{9,8},{10,9... | collective-permute-start | bytes 589832 | tf_op jit(solution)/shard_map/ppermute | solution.py:32
  25.5 6.7 %collective-permute-start.9 = (bf16[64,1536]{1,0:T(8,128)(2,1)S(1)}, bf16[64,1536]{1,0:T(8,128)(2,1)S(1)}, u32[]{:S(2)}, u32[]{:S(2)}) collective-permute-start(bf16[64,1536]{1,0:T(8,128)(2,1)S(1)} %collective-permute-done.7), channel_id=1, source_target_pairs={{0,15},{1,0},{2,1},{3,2},{4,3},{5,4},{6,5},{7,6},{8,7},{9,8},{10,9... | collective-permute-start | bytes 589832 | tf_op jit(solution)/shard_map/ppermute | solution.py:32
  33.3 6.8 %collective-permute-start.11 = (bf16[64,1536]{1,0:T(8,128)(2,1)S(1)}, bf16[64,1536]{1,0:T(8,128)(2,1)S(1)}, u32[]{:S(2)}, u32[]{:S(2)}) collective-permute-start(bf16[64,1536]{1,0:T(8,128)(2,1)S(1)} %collective-permute-done.9), channel_id=1, source_target_pairs={{0,15},{1,0},{2,1},{3,2},{4,3},{5,4},{6,5},{7,6},{8,7},{9,8},{10,9... | collective-permute-start | bytes 589832 | tf_op jit(solution)/shard_map/ppermute | solution.py:32
  41.2 6.8 %collective-permute-start.13 = (bf16[64,1536]{1,0:T(8,128)(2,1)S(1)}, bf16[64,1536]{1,0:T(8,128)(2,1)S(1)}, u32[]{:S(2)}, u32[]{:S(2)}) collective-permute-start(bf16[64,1536]{1,0:T(8,128)(2,1)S(1)} %collective-permute-done.11), channel_id=1, source_target_pairs={{0,15},{1,0},{2,1},{3,2},{4,3},{5,4},{6,5},{7,6},{8,7},{9,8},{10,9... | collective-permute-start | bytes 589832 | tf_op jit(solution)/shard_map/ppermute | solution.py:32
  48.1 5.6 %collective-permute-done.12 = bf16[64,1536]{1,0:T(8,128)(2,1)S(1)} collective-permute-done((bf16[64,1536]{1,0:T(8,128)(2,1)S(1)}, bf16[64,1536]{1,0:T(8,128)(2,1)S(1)}, u32[]{:S(2)}, u32[]{:S(2)}) %collective-permute-start.12) | collective-permute-done | bytes 196640 | tf_op jit(solution)/shard_map/ppermute | solution.py:26
  53.7 7.7 %collective-permute-done.14 = bf16[64,1536]{1,0:T(8,128)(2,1)S(1)} collective-permute-done((bf16[64,1536]{1,0:T(8,128)(2,1)S(1)}, bf16[64,1536]{1,0:T(8,128)(2,1)S(1)}, u32[]{:S(2)}, u32[]{:S(2)}) %collective-permute-start.14) | collective-permute-done | bytes 196640 | tf_op jit(solution)/shard_map/ppermute | solution.py:26
  61.5 3.0 %fusion.30 = bf16[4,128,1536]{2,1,0:T(8,128)(2,1)} fusion(bf16[1024,1536]{1,0:T(8,128)(2,1)S(1)} %constant_dynamic-update-slice_fusion, bf16[4,128,1024]{2,1,0:T(8,128)(2,1)S(1)} %mul.161, bf16[4,1024]{1,0:T(4,128)(2,1)S(1)} %bitcast.76), kind=kOutput, calls=%fused_computation.47 | convolution fusion | flops 1611923456 | bytes 5775360 | tf_op jit(solution)/shard_map/bop,pd->bod/dot_general | solution.py:83
  64.5 8.8 %collective-permute-start.16 = (bf16[4,128,1536]{2,1,0:T(8,128)(2,1)}, bf16[4,128,1536]{2,1,0:T(8,128)(2,1)}, u32[]{:S(2)}, u32[]{:S(2)}) collective-permute-start(bf16[4,128,1536]{2,1,0:T(8,128)(2,1)} %fusion.30), channel_id=1, source_target_pairs={{1,0},{2,1},{3,2},{4,3},{5,4},{6,5},{7,6},{8,7},{9,8},{10,9},{11,1... | collective-permute-start | bytes 4718600 | tf_op jit(solution)/shard_map/ppermute | solution.py:47
  73.2 2.1 collective-permute-start.15
  78.1 1.9 copy.33
  80.0 6.5 %collective-permute-done.16 = bf16[4,128,1536]{2,1,0:T(8,128)(2,1)} collective-permute-done((bf16[4,128,1536]{2,1,0:T(8,128)(2,1)}, bf16[4,128,1536]{2,1,0:T(8,128)(2,1)}, u32[]{:S(2)}, u32[]{:S(2)}) %collective-permute-start.16) | collective-permute-done | bytes 1572896 | tf_op jit(solution)/shard_map/ppermute | solution.py:47
  86.5 8.6 %collective-permute-done.15 = bf16[4,128,1536]{2,1,0:T(8,128)(2,1)} collective-permute-done((bf16[4,128,1536]{2,1,0:T(8,128)(2,1)}, bf16[4,128,1536]{2,1,0:T(8,128)(2,1)}, u32[]{:S(2)}, u32[]{:S(2)}) %collective-permute-start.15) | collective-permute-done | bytes 1572896 | tf_op jit(solution)/shard_map/ppermute | solution.py:46
  95.1 5.7 %multiply_reduce_fusion = (f32[12,128]{1,0:T(8,128)S(1)}, bf16[12,128,1536]{2,1,0:T(8,128)(2,1)}) fusion(bf16[4,128,1536]{2,1,0:T(8,128)(2,1)} %collective-permute-done.16, bf16[4,128,1536]{2,1,0:T(8,128)(2,1)} %fusion.30, bf16[4,128,1536]{2,1,0:T(8,128)(2,1)} %collective-permute-done.15), kind=kLoop, calls=%fused_computation.36 | loop fusion | flops 11794944 | bytes 9443328 | tf_op jit(solution)/shard_map/reduce_sum | solution.py:54
  100.8 2.6 %copy.34 = bf16[4,128,1536]{1,2,0:T(8,128)(2,1)} copy(bf16[4,128,1536]{2,1,0:T(8,128)(2,1)} %collective-permute-done.16) | data formatting | bytes 3145728 | tf_op jit(solution)/shard_map/ppermute | solution.py:47
  103.3 2.6 %copy.32 = bf16[4,128,1536]{1,2,0:T(8,128)(2,1)} copy(bf16[4,128,1536]{2,1,0:T(8,128)(2,1)} %collective-permute-done.15) | data formatting | bytes 3145728 | tf_op jit(solution)/shard_map/ppermute | solution.py:46
  105.9 3.7 %fusion.26 = bf16[12,24,64,128]{3,2,1,0:T(8,128)(2,1)S(1)} fusion(bf16[4,128,24,64]{1,3,2,0:T(8,128)(2,1)} %bitcast.73, bf16[4,128,24,64]{1,3,2,0:T(8,128)(2,1)S(1)} %bitcast.72, bf16[4,128,24,64]{1,3,2,0:T(8,128)(2,1)} %bitcast.74, f32[24,64]{1,0:T(8,128)S(1)} %mul.186, f32[12,128]{1,0:T(8,128)S(1)} %add_rsqrt_fusion), kind=kLoop, calls=%fused_computation.37 | loop fusion | flops 14155776 | bytes 9449472 | tf_op jit(solution)/shard_map/transpose | solution.py:91
  109.6 6.9 %copy.37 = bf16[12,24,64,128]{3,0,2,1:T(8,128)(2,1)} copy(bf16[12,24,64,128]{3,2,1,0:T(8,128)(2,1)S(1)} %fusion.26) | data formatting | bytes 9437184
  116.5 9.1 %copy.43 = bf16[12,128,1536]{1,0,2:T(8,128)(2,1)} copy(bf16[12,128,1536]{2,1,0:T(8,128)(2,1)} %get-tuple-element.287) | data formatting | bytes 9437184 | tf_op jit(solution)/shard_map/transpose | solution.py:92
  125.6 78.2 %while.18 = (s32[]{:T(128)}, f32[4,24,128]{2,1,0:T(8,128)S(1)}, f32[4,24,128]{2,1,0:T(8,128)S(1)}, f32[4,24,64,128]{3,2,1,0:T(8,128)}, s32[4]{0:T(128)S(1)}, /*i...) while((s32[]{:T(128)}, f32[4,24,128]{2,1,0:T(8,128)S(1)}, ...), condition=%wide.region_5.6_spmd.clone, body=%wide.region_1.5_spmd.clone.sunk | while | flops 461698304 | bytes 87296416 | solution.py:136
  125.9 4.0 %convolution_convert_fusion.5 = bf16[4,24,64,128]{3,0,2,1:T(4,128)(2,1)S(1)} fusion(bf16[12,24,64,128]{3,0,2,1:T(8,128)(2,1)} %get-tuple-element.394, s32[4]{0:T(128)S(1)} %dynamic-slice_bitcast_fusion.2), kind=kOutput, calls=%fused_computation.14.clone.1 | convolution fusion | flops 19660848 | bytes 6291472 | tf_op jit(solution)/shard_map/while/body/eval_jaxpr/tn,nhdk->thdk/dot_general | solution.py:108
  135.3 1.8 fusion.63
  139.0 4.0 %convolution_convert_fusion.5 = bf16[4,24,64,128]{3,0,2,1:T(4,128)(2,1)S(1)} fusion(bf16[12,24,64,128]{3,0,2,1:T(8,128)(2,1)} %get-tuple-element.394, s32[4]{0:T(128)S(1)} %dynamic-slice_bitcast_fusion.2), kind=kOutput, calls=%fused_computation.14.clone.1 | convolution fusion | flops 19660848 | bytes 6291472 | tf_op jit(solution)/shard_map/while/body/eval_jaxpr/tn,nhdk->thdk/dot_general | solution.py:108
  152.0 4.0 %convolution_convert_fusion.5 = bf16[4,24,64,128]{3,0,2,1:T(4,128)(2,1)S(1)} fusion(bf16[12,24,64,128]{3,0,2,1:T(8,128)(2,1)} %get-tuple-element.394, s32[4]{0:T(128)S(1)} %dynamic-slice_bitcast_fusion.2), kind=kOutput, calls=%fused_computation.14.clone.1 | convolution fusion | flops 19660848 | bytes 6291472 | tf_op jit(solution)/shard_map/while/body/eval_jaxpr/tn,nhdk->thdk/dot_general | solution.py:108
  165.0 4.0 %convolution_convert_fusion.5 = bf16[4,24,64,128]{3,0,2,1:T(4,128)(2,1)S(1)} fusion(bf16[12,24,64,128]{3,0,2,1:T(8,128)(2,1)} %get-tuple-element.394, s32[4]{0:T(128)S(1)} %dynamic-slice_bitcast_fusion.2), kind=kOutput, calls=%fused_computation.14.clone.1 | convolution fusion | flops 19660848 | bytes 6291472 | tf_op jit(solution)/shard_map/while/body/eval_jaxpr/tn,nhdk->thdk/dot_general | solution.py:108
  178.1 4.0 %convolution_convert_fusion.5 = bf16[4,24,64,128]{3,0,2,1:T(4,128)(2,1)S(1)} fusion(bf16[12,24,64,128]{3,0,2,1:T(8,128)(2,1)} %get-tuple-element.394, s32[4]{0:T(128)S(1)} %dynamic-slice_bitcast_fusion.2), kind=kOutput, calls=%fused_computation.14.clone.1 | convolution fusion | flops 19660848 | bytes 6291472 | tf_op jit(solution)/shard_map/while/body/eval_jaxpr/tn,nhdk->thdk/dot_general | solution.py:108
  191.1 4.0 %convolution_convert_fusion.5 = bf16[4,24,64,128]{3,0,2,1:T(4,128)(2,1)S(1)} fusion(bf16[12,24,64,128]{3,0,2,1:T(8,128)(2,1)} %get-tuple-element.394, s32[4]{0:T(128)S(1)} %dynamic-slice_bitcast_fusion.2), kind=kOutput, calls=%fused_computation.14.clone.1 | convolution fusion | flops 19660848 | bytes 6291472 | tf_op jit(solution)/shard_map/while/body/eval_jaxpr/tn,nhdk->thdk/dot_general | solution.py:108
  203.9 2.5 %fusion.35 = bf16[4,128,24,64]{1,3,2,0:T(8,128)(2,1)S(1)} fusion(f32[4,24,64,128]{3,2,1,0:T(8,128)} %get-tuple-element.205, f32[4,24,128]{2,1,0:T(8,128)S(1)} %get-tuple-element.206), kind=kLoop, calls=%fused_computation.50 | loop fusion | flops 1572864 | bytes 4767744 | tf_op jit(solution)/shard_map/transpose | solution.py:140
  207.9 3.0 %multiply_reduce_fusion.1 = (f32[512]{0:T(512)S(1)}, f32[512,1536]{1,0:T(8,128)S(1)}) fusion(bf16[1536,1536]{1,0:T(8,128)(2,1)S(1)} %copy-done.12, bf16[192,8,4,128]{3,2,1,0:T(4,128)(2,1)S(1)} %bitcast.75, bf16[512,1536]{1,0:T(8,128)(2,1)S(1)} %copy-done.6), kind=kOutput, calls=%fused_computation.45 | convolution fusion | flops 2419064320 | bytes 11012096 | tf_op jit(solution)/shard_map/dot_general | solution.py:143
  (183 shorter events, 67.4 us)
Async XLA Ops:
  0.0 77.4 %copy-start = (s32[64]{0:T(128)S(1)}, s32[64]{0:T(128)}, u32[]{:S(2)}) copy-start(s32[64]{0:T(128)} %param.21) | copy-start | bytes 772
  0.0 6.2 %collective-permute-start.1 = (bf16[64,1536]{1,0:T(8,128)(2,1)}, bf16[64,1536]{1,0:T(8,128)(2,1)S(1)}, u32[]{:S(2)}, u32[]{:S(2)}) collective-permute-start(bf16[64,1536]{1,0:T(8,128)(2,1)} %param.19), channel_id=1, source_target_pairs={{0,15},{1,0},{2,1},{3,2},{4,3},{5,4},{6,5},{7,6},{8,7},{9,8},{10,9... | collective-permute-start | bytes 589832 | tf_op jit(solution)/shard_map/ppermute | solution.py:32
  0.0 9.0 %collective-permute-start = (bf16[64,1536]{1,0:T(8,128)(2,1)}, bf16[64,1536]{1,0:T(8,128)(2,1)S(1)}, u32[]{:S(2)}, u32[]{:S(2)}) collective-permute-start(bf16[64,1536]{1,0:T(8,128)(2,1)} %param.19), channel_id=1, source_target_pairs={{0,1},{1,2},{2,3},{3,4},{4,5},{5,6},{6,7},{7,8},{8,9},{9,10},{10,1... | collective-permute-start | bytes 589832 | tf_op jit(solution)/shard_map/ppermute | solution.py:26
  6.2 7.2 %collective-permute-start.3 = (bf16[64,1536]{1,0:T(8,128)(2,1)S(1)}, bf16[64,1536]{1,0:T(8,128)(2,1)S(1)}, u32[]{:S(2)}, u32[]{:S(2)}) collective-permute-start(bf16[64,1536]{1,0:T(8,128)(2,1)S(1)} %collective-permute-done.1), channel_id=1, source_target_pairs={{0,15},{1,0},{2,1},{3,2},{4,3},{5,4},{6,5},{7,6},{8,7},{9,8},{10,9... | collective-permute-start | bytes 589832 | tf_op jit(solution)/shard_map/ppermute | solution.py:32
  9.0 7.7 %collective-permute-start.2 = (bf16[64,1536]{1,0:T(8,128)(2,1)S(1)}, bf16[64,1536]{1,0:T(8,128)(2,1)S(1)}, u32[]{:S(2)}, u32[]{:S(2)}) collective-permute-start(bf16[64,1536]{1,0:T(8,128)(2,1)S(1)} %collective-permute-done), channel_id=1, source_target_pairs={{0,1},{1,2},{2,3},{3,4},{4,5},{5,6},{6,7},{7,8},{8,9},{9,10},{10,1... | collective-permute-start | bytes 589832 | tf_op jit(solution)/shard_map/ppermute | solution.py:26
  13.4 5.1 %collective-permute-start.5 = (bf16[64,1536]{1,0:T(8,128)(2,1)S(1)}, bf16[64,1536]{1,0:T(8,128)(2,1)S(1)}, u32[]{:S(2)}, u32[]{:S(2)}) collective-permute-start(bf16[64,1536]{1,0:T(8,128)(2,1)S(1)} %collective-permute-done.3), channel_id=1, source_target_pairs={{0,15},{1,0},{2,1},{3,2},{4,3},{5,4},{6,5},{7,6},{8,7},{9,8},{10,9... | collective-permute-start | bytes 589832 | tf_op jit(solution)/shard_map/ppermute | solution.py:32
  16.7 7.8 %collective-permute-start.4 = (bf16[64,1536]{1,0:T(8,128)(2,1)S(1)}, bf16[64,1536]{1,0:T(8,128)(2,1)S(1)}, u32[]{:S(2)}, u32[]{:S(2)}) collective-permute-start(bf16[64,1536]{1,0:T(8,128)(2,1)S(1)} %collective-permute-done.2), channel_id=1, source_target_pairs={{0,1},{1,2},{2,3},{3,4},{4,5},{5,6},{6,7},{7,8},{8,9},{9,10},{10,1... | collective-permute-start | bytes 589832 | tf_op jit(solution)/shard_map/ppermute | solution.py:26
  18.5 7.1 %collective-permute-start.7 = (bf16[64,1536]{1,0:T(8,128)(2,1)S(1)}, bf16[64,1536]{1,0:T(8,128)(2,1)S(1)}, u32[]{:S(2)}, u32[]{:S(2)}) collective-permute-start(bf16[64,1536]{1,0:T(8,128)(2,1)S(1)} %collective-permute-done.5), channel_id=1, source_target_pairs={{0,15},{1,0},{2,1},{3,2},{4,3},{5,4},{6,5},{7,6},{8,7},{9,8},{10,9... | collective-permute-start | bytes 589832 | tf_op jit(solution)/shard_map/ppermute | solution.py:32
  24.5 7.8 %collective-permute-start.6 = (bf16[64,1536]{1,0:T(8,128)(2,1)S(1)}, bf16[64,1536]{1,0:T(8,128)(2,1)S(1)}, u32[]{:S(2)}, u32[]{:S(2)}) collective-permute-start(bf16[64,1536]{1,0:T(8,128)(2,1)S(1)} %collective-permute-done.4), channel_id=1, source_target_pairs={{0,1},{1,2},{2,3},{3,4},{4,5},{5,6},{6,7},{7,8},{8,9},{9,10},{10,1... | collective-permute-start | bytes 589832 | tf_op jit(solution)/shard_map/ppermute | solution.py:26
  25.5 7.8 %collective-permute-start.9 = (bf16[64,1536]{1,0:T(8,128)(2,1)S(1)}, bf16[64,1536]{1,0:T(8,128)(2,1)S(1)}, u32[]{:S(2)}, u32[]{:S(2)}) collective-permute-start(bf16[64,1536]{1,0:T(8,128)(2,1)S(1)} %collective-permute-done.7), channel_id=1, source_target_pairs={{0,15},{1,0},{2,1},{3,2},{4,3},{5,4},{6,5},{7,6},{8,7},{9,8},{10,9... | collective-permute-start | bytes 589832 | tf_op jit(solution)/shard_map/ppermute | solution.py:32
  32.2 7.9 %collective-permute-start.8 = (bf16[64,1536]{1,0:T(8,128)(2,1)S(1)}, bf16[64,1536]{1,0:T(8,128)(2,1)S(1)}, u32[]{:S(2)}, u32[]{:S(2)}) collective-permute-start(bf16[64,1536]{1,0:T(8,128)(2,1)S(1)} %collective-permute-done.6), channel_id=1, source_target_pairs={{0,1},{1,2},{2,3},{3,4},{4,5},{5,6},{6,7},{7,8},{8,9},{9,10},{10,1... | collective-permute-start | bytes 589832 | tf_op jit(solution)/shard_map/ppermute | solution.py:26
  33.3 7.9 %collective-permute-start.11 = (bf16[64,1536]{1,0:T(8,128)(2,1)S(1)}, bf16[64,1536]{1,0:T(8,128)(2,1)S(1)}, u32[]{:S(2)}, u32[]{:S(2)}) collective-permute-start(bf16[64,1536]{1,0:T(8,128)(2,1)S(1)} %collective-permute-done.9), channel_id=1, source_target_pairs={{0,15},{1,0},{2,1},{3,2},{4,3},{5,4},{6,5},{7,6},{8,7},{9,8},{10,9... | collective-permute-start | bytes 589832 | tf_op jit(solution)/shard_map/ppermute | solution.py:32
  40.1 7.9 %collective-permute-start.10 = (bf16[64,1536]{1,0:T(8,128)(2,1)S(1)}, bf16[64,1536]{1,0:T(8,128)(2,1)S(1)}, u32[]{:S(2)}, u32[]{:S(2)}) collective-permute-start(bf16[64,1536]{1,0:T(8,128)(2,1)S(1)} %collective-permute-done.8), channel_id=1, source_target_pairs={{0,1},{1,2},{2,3},{3,4},{4,5},{5,6},{6,7},{7,8},{8,9},{9,10},{10,1... | collective-permute-start | bytes 589832 | tf_op jit(solution)/shard_map/ppermute | solution.py:26
  41.2 12.5 %collective-permute-start.13 = (bf16[64,1536]{1,0:T(8,128)(2,1)S(1)}, bf16[64,1536]{1,0:T(8,128)(2,1)S(1)}, u32[]{:S(2)}, u32[]{:S(2)}) collective-permute-start(bf16[64,1536]{1,0:T(8,128)(2,1)S(1)} %collective-permute-done.11), channel_id=1, source_target_pairs={{0,15},{1,0},{2,1},{3,2},{4,3},{5,4},{6,5},{7,6},{8,7},{9,8},{10,9... | collective-permute-start | bytes 589832 | tf_op jit(solution)/shard_map/ppermute | solution.py:32
  48.0 5.6 %collective-permute-start.12 = (bf16[64,1536]{1,0:T(8,128)(2,1)S(1)}, bf16[64,1536]{1,0:T(8,128)(2,1)S(1)}, u32[]{:S(2)}, u32[]{:S(2)}) collective-permute-start(bf16[64,1536]{1,0:T(8,128)(2,1)S(1)} %collective-permute-done.10), channel_id=1, source_target_pairs={{0,1},{1,2},{2,3},{3,4},{4,5},{5,6},{6,7},{7,8},{8,9},{9,10},{10,1... | collective-permute-start | bytes 589832 | tf_op jit(solution)/shard_map/ppermute | solution.py:26
  53.7 7.8 %collective-permute-start.14 = (bf16[64,1536]{1,0:T(8,128)(2,1)S(1)}, bf16[64,1536]{1,0:T(8,128)(2,1)S(1)}, u32[]{:S(2)}, u32[]{:S(2)}) collective-permute-start(bf16[64,1536]{1,0:T(8,128)(2,1)S(1)} %collective-permute-done.12), channel_id=1, source_target_pairs={{0,1},{1,2},{2,3},{3,4},{4,5},{5,6},{6,7},{7,8},{8,9},{9,10},{10,1... | collective-permute-start | bytes 589832 | tf_op jit(solution)/shard_map/ppermute | solution.py:26
  61.5 13.9 %copy-start.11 = (s32[4,6]{1,0:T(4,128)S(1)}, s32[4,6]{1,0:T(4,128)}, u32[]{:S(2)}) copy-start(s32[4,6]{1,0:T(4,128)} %param.22) | copy-start | bytes 292
  61.5 14.0 %copy-start.10 = (f32[1536]{0:T(1024)S(1)}, f32[1536]{0:T(1024)}, u32[]{:S(2)}) copy-start(f32[1536]{0:T(1024)} %param.15) | copy-start | bytes 18436
  61.5 14.1 %copy-start.5 = (bf16[512,1536]{1,0:T(8,128)(2,1)S(1)}, bf16[512,1536]{1,0:T(8,128)(2,1)}, u32[]{:S(2)}) copy-start(bf16[512,1536]{1,0:T(8,128)(2,1)} %param.13) | copy-start | bytes 4718596
  61.5 14.0 %copy-start.8 = (f32[1536]{0:T(1024)S(1)}, f32[1536]{0:T(1024)}, u32[]{:S(2)}) copy-start(f32[1536]{0:T(1024)} %param.14) | copy-start | bytes 18436
  64.5 22.0 %collective-permute-start.16 = (bf16[4,128,1536]{2,1,0:T(8,128)(2,1)}, bf16[4,128,1536]{2,1,0:T(8,128)(2,1)}, u32[]{:S(2)}, u32[]{:S(2)}) collective-permute-start(bf16[4,128,1536]{2,1,0:T(8,128)(2,1)} %fusion.30), channel_id=1, source_target_pairs={{1,0},{2,1},{3,2},{4,3},{5,4},{6,5},{7,6},{8,7},{9,8},{10,9},{11,1... | collective-permute-start | bytes 4718600 | tf_op jit(solution)/shard_map/ppermute | solution.py:47
  73.2 21.8 %collective-permute-start.15 = (bf16[4,128,1536]{2,1,0:T(8,128)(2,1)}, bf16[4,128,1536]{2,1,0:T(8,128)(2,1)}, u32[]{:S(2)}, u32[]{:S(2)}) collective-permute-start(bf16[4,128,1536]{2,1,0:T(8,128)(2,1)} %fusion.30), channel_id=1, source_target_pairs={{0,1},{1,2},{2,3},{3,4},{4,5},{5,6},{6,7},{7,8},{8,9},{9,10},{10,1... | collective-permute-start | bytes 4718600 | tf_op jit(solution)/shard_map/ppermute | solution.py:46
  116.5 9.1 %copy-start.13 = (s32[4]{0:T(128)S(1)}, s32[4]{0:T(128)}, u32[]{:S(2)}) copy-start(s32[4]{0:T(128)} %param.23) | copy-start | bytes 52
  125.9 4.6 %copy-start.2 = (bf16[12,24,64,128]{3,0,2,1:T(8,128)(2,1)S(1)}, bf16[12,24,64,128]{3,0,2,1:T(8,128)(2,1)}, u32[]{:S(2)}) copy-start(bf16[12,24,64,128]{3,0,2,1:T(8,128)(2,1)} %get-tuple-element.392) | copy-start | bytes 14155780 | tf_op jit(solution)/shard_map/while
  139.0 4.6 %copy-start.2 = (bf16[12,24,64,128]{3,0,2,1:T(8,128)(2,1)S(1)}, bf16[12,24,64,128]{3,0,2,1:T(8,128)(2,1)}, u32[]{:S(2)}) copy-start(bf16[12,24,64,128]{3,0,2,1:T(8,128)(2,1)} %get-tuple-element.392) | copy-start | bytes 14155780 | tf_op jit(solution)/shard_map/while
  152.0 4.6 %copy-start.2 = (bf16[12,24,64,128]{3,0,2,1:T(8,128)(2,1)S(1)}, bf16[12,24,64,128]{3,0,2,1:T(8,128)(2,1)}, u32[]{:S(2)}) copy-start(bf16[12,24,64,128]{3,0,2,1:T(8,128)(2,1)} %get-tuple-element.392) | copy-start | bytes 14155780 | tf_op jit(solution)/shard_map/while
  165.0 4.6 %copy-start.2 = (bf16[12,24,64,128]{3,0,2,1:T(8,128)(2,1)S(1)}, bf16[12,24,64,128]{3,0,2,1:T(8,128)(2,1)}, u32[]{:S(2)}) copy-start(bf16[12,24,64,128]{3,0,2,1:T(8,128)(2,1)} %get-tuple-element.392) | copy-start | bytes 14155780 | tf_op jit(solution)/shard_map/while
  178.1 4.6 %copy-start.2 = (bf16[12,24,64,128]{3,0,2,1:T(8,128)(2,1)S(1)}, bf16[12,24,64,128]{3,0,2,1:T(8,128)(2,1)}, u32[]{:S(2)}) copy-start(bf16[12,24,64,128]{3,0,2,1:T(8,128)(2,1)} %get-tuple-element.392) | copy-start | bytes 14155780 | tf_op jit(solution)/shard_map/while
  191.1 4.6 %copy-start.2 = (bf16[12,24,64,128]{3,0,2,1:T(8,128)(2,1)S(1)}, bf16[12,24,64,128]{3,0,2,1:T(8,128)(2,1)}, u32[]{:S(2)}) copy-start(bf16[12,24,64,128]{3,0,2,1:T(8,128)(2,1)} %get-tuple-element.392) | copy-start | bytes 14155780 | tf_op jit(solution)/shard_map/while
  203.9 4.0 %copy-start.6 = (bf16[512,1536]{1,0:T(8,128)(2,1)S(1)}, bf16[512,1536]{1,0:T(8,128)(2,1)}, u32[]{:S(2)}) copy-start(bf16[512,1536]{1,0:T(8,128)(2,1)} %param.13) | copy-start | bytes 4718596
  203.9 4.0 %copy-start.12 = (bf16[1536,1536]{1,0:T(8,128)(2,1)S(1)}, bf16[1536,1536]{1,0:T(8,128)(2,1)}, u32[]{:S(2)}) copy-start(bf16[1536,1536]{1,0:T(8,128)(2,1)} %param.17) | copy-start | bytes 14155780
  207.9 4.5 %copy-start.1 = (s32[64]{0:T(128)S(1)}, s32[64]{0:T(128)}, u32[]{:S(2)}) copy-start(s32[64]{0:T(128)} %param.21) | copy-start | bytes 772
  (14 other events, 26.0 us)
